TPU v7x, 32 devices: a whole 2x2x4 slice. The times are simulated.
32 devices in a mesh: req: 8 (over y, x, core), tp: 4 (over z).
Axes of the slice: x: 2, y: 2, z: 4, core: 2. Of those that a mesh axis runs over, the one named last changes fastest.
Arguments:
- final_states: float32 [16384, 1024], P('req'), may hold values from -50 to 50
- norm_gain: float32 [1024], replicated, may hold values from 0.1 to 1.9
- embedding: bfloat16 [32768, 1024], P('tp'), may hold values from -2 to 2
- targets: int32 [16384], P('req'), may hold values from 0 to 32767
- deal: int32 [8192], P('req'), may hold values from 0 to 16383, as said below
Outputs:
- logprob: float32 [16384], P('req')
- entropy: float32 [16384], P('req')
Inputs may be any that keep to these rules, and one draw needn't show every extreme that they name: Every owned row is named at most once. The rows named of each owner device are a prefix of its 2048 rows (its sequence's live tokens), between 128 and 2048 rows long, and some owner device is named in full; the rest is padding. Each owner's live rows are dealt over all req devices, its own device included. Along each device's 8192 // 8 positions, in order, the owner device number deal // 2048 never decreases. At most 256 positions of one device name rows of one owner device, and some device reaches 256.
All inputs are finite; a program needn't handle non-finite values.
Results may differ from a plain program's by a relative error of at most 0.0031.
Values sent between devices are 32-bit elements; how exact they have to be, the bound alone decides.
No kernel may reach another device: no remote copies, remote signals or barrier semaphores. Data moves between devices by JAX's collectives and lax.ppermute only.
A program may use at most 128 MiB of HBM per device.

v0:
```python
import jax
import jax.numpy as jnp
from jax import lax
from jax.sharding import PartitionSpec as P


def rms_normed(states, norm_gain):
    mean_square = jnp.mean(states * states, axis=1, keepdims=True)
    return (states * lax.rsqrt(mean_square + 1e-06) * norm_gain[None, :]).astype(jnp.bfloat16)


def body(final_states, norm_gain, embedding, targets, deal):
    owners = lax.axis_size("req")
    own_rows = final_states.shape[0]
    capacity = own_rows // owners
    positions = deal.shape[0]
    shard_cols = embedding.shape[0]
    vocab_start = lax.axis_index("tp") * shard_cols
    source = deal // own_rows
    local_row = deal % own_rows
    member = (source[:, None] == jnp.arange(owners, dtype=jnp.int32)[None, :]).astype(jnp.int32)
    counts = jnp.sum(member, axis=0)
    starts = jnp.cumsum(counts) - counts
    offset = jnp.arange(positions, dtype=jnp.int32) - jnp.sum(member * starts[None, :], axis=1)
    slot_index = source * capacity + offset
    asked_rows = jnp.full((owners * capacity,), -1, jnp.int32).at[slot_index].set(local_row)
    wanted = lax.all_to_all(asked_rows, "req", split_axis=0, concat_axis=0, tiled=True)
    is_live = wanted >= 0
    picked = jnp.where(is_live, wanted, 0)
    outgoing_rows = jnp.where(is_live[:, None], final_states[picked], 0.0)
    arrived = lax.all_to_all(outgoing_rows, "req", split_axis=0, concat_axis=0, tiled=True)
    scored_rows = arrived[slot_index]
    owned_normed = rms_normed(final_states, norm_gain)
    in_shard_id = targets - vocab_start
    inside = (in_shard_id >= 0) & (in_shard_id < shard_cols)
    target_rows = embedding[jnp.clip(in_shard_id, 0, shard_cols - 1)]
    target_term = jnp.einsum(
        "rd,rd->r", owned_normed, target_rows, preferred_element_type=jnp.float32
    )
    owner_chosen = lax.psum(jnp.where(inside, target_term, 0.0), "tp")
    normed = rms_normed(scored_rows, norm_gain)
    logits = lax.dot_general(
        normed, embedding, (((1,), (1,)), ((), ())), preferred_element_type=jnp.float32
    )
    local_peak = jnp.max(logits, axis=1)
    row_peak = lax.pmax(local_peak, "tp")
    weights = jnp.exp(logits - row_peak[:, None])
    local_sums = jnp.stack((jnp.sum(weights, axis=1), jnp.sum(weights * logits, axis=1)))
    sums_all = lax.psum(local_sums, "tp")
    log_total = row_peak + jnp.log(sums_all[0])
    expected = sums_all[1] / sums_all[0]
    result_rows = jnp.stack((log_total, expected))
    outgoing = jnp.zeros((2, owners * capacity), jnp.float32).at[:, slot_index].set(result_rows)
    returned = lax.all_to_all(outgoing, "req", split_axis=1, concat_axis=1, tiled=True)
    home_row = jnp.where(is_live, wanted, own_rows)

    def to_owner(values):
        return jnp.zeros((own_rows,), jnp.float32).at[home_row].set(values, mode="drop")

    live_rows = to_owner(jnp.ones((owners * capacity,), jnp.float32))
    log_owned = to_owner(returned[0])
    expected_owned = to_owner(returned[1])
    logprob = (owner_chosen - log_owned) * live_rows
    entropy = log_owned - expected_owned
    return (logprob, entropy)


def solution(mesh):
    return jax.shard_map(
        body,
        mesh=mesh,
        in_specs=(P("req", None), P(), P("tp", None), P("req"), P("req")),
        out_specs=(P("req"), P("req")),
        check_vma=False,
    )
```

profile of v0, /device:TPU:0, one launch (start us, length us, event | category | flops | bytes accessed | tf_op | source)
XLA Modules:
  0.0 251.2 jit_solution(6436493523009157254)
XLA Ops:
  0.6 0.7 add_select_fusion.1
  1.3 0.1 convert_reduce_fusion
  1.5 0.2 reduce-window.8
  1.6 0.1 select_reduce_fusion
  1.7 0.7 broadcast_clamp_fusion.1
  2.4 4.3 %scatter_custom_fusion = s32[2048]{0:T(1024)S(1)} fusion(s32[1024]{0:T(1024)S(1)} %get-tuple-element.7, s32[1024]{0:T(1024)S(1)} %get-tuple-element.16, s32[]{:T(128)} %constant.57.clone.1), kind=kCustom, calls=%fused_computation.49 | custom fusion | bytes 8196 | tf_op jit(solution)/shard_map/scatter | solution.py:26
  6.8 9.7 %all_to_all.30 = s32[8,256,1]{1,2,0:T(1,128)S(1)} all-to-all(s32[8,256,1]{1,2,0:T(1,128)S(1)} %bitcast.25), channel_id=1, replica_groups=mesh['req'=8,'tp'=4] {'req'}, dimensions={0} | all-to-all | bytes 16384 | tf_op jit(solution)/shard_map/all_to_all | solution.py:27
  16.5 15.1 %gather_fusion.1 = f32[2048,1024]{1,0:T(8,128)} fusion(f32[2048,1024]{1,0:T(8,128)} %param.5, s32[2048]{0:T(1024)S(1)} %broadcast_clamp_fusion), kind=kCustom, calls=%fused_computation.1 | custom fusion | bytes 16785408 | tf_op jit(solution)/shard_map/gather | solution.py:30
  31.6 5.8 %broadcast_select_fusion = f32[8,256,1024]{2,1,0:T(8,128)} fusion(f32[8,256,1024]{2,1,0:T(8,128)} %bitcast.21, pred[8,256]{1,0:T(8,128)(4,1)S(1)} %fusion.8), kind=kLoop, calls=%fused_computation.17 | loop fusion | flops 2097152 | bytes 16779264 | tf_op jit(solution)/shard_map/jit(_where)/select_n | solution.py:30
  37.4 0.0 copy-start.1
  37.4 5.3 %all-to-all-start.1 = ((f32[8,256,1024]{2,1,0:T(8,128)}), f32[8,256,1024]{2,1,0:T(8,128)}, u32[]{:S(2)}, u32[]{:S(2)}) async-start(f32[8,256,1024]{2,1,0:T(8,128)} %broadcast_select_fusion), calls=%async_computation.1 | async-start | bytes 16777216 | tf_op jit(solution)/shard_map/all_to_all | solution.py:31
  42.7 0.0 copy-done.1
  42.7 18.9 %gather_fusion = bf16[2048,1024]{1,0:T(8,128)(2,1)} fusion(bf16[8192,1024]{1,0:T(8,128)(2,1)} %param.7, s32[2048]{0:T(1024)S(1)} %fusion.7), kind=kCustom, calls=%fused_computation | custom fusion | bytes 8396800 | tf_op jit(solution)/shard_map/gather | solution.py:36
  61.7 0.0 copy-start
  61.7 0.0 copy-start.2
  61.7 4.1 %multiply_reduce_fusion.1 = f32[2048]{0:T(1024)S(1)} fusion(f32[2048,1024]{1,0:T(8,128)} %param.5), kind=kLoop, calls=%fused_computation.14 | loop fusion | flops 4192256 | bytes 8396800 | tf_op jit(solution)/shard_map/reduce_sum | solution.py:8
  65.8 0.4 copy-done
  66.2 0.0 copy-done.2
  66.2 4.4 %fusion.1 = f32[2048]{0:T(1024)S(1)} fusion(bf16[2048,1024]{1,0:T(8,128)(2,1)S(1)} %copy-done, f32[2048,1024]{1,0:T(8,128)} %param.5, f32[1024]{0:T(1024)S(1)} %copy-done.2, f32[2048]{0:T(1024)S(1)} %add_rsqrt_fusion), kind=kLoop, calls=%fused_computation.12 | loop fusion | flops 14678016 | bytes 12603392 | tf_op jit(solution)/shard_map/rd,rd->r/dot_general | solution.py:37
  70.6 66.0 %all-to-all-done.1 = f32[8,256,1024]{2,1,0:T(8,128)} async-done(((f32[8,256,1024]{2,1,0:T(8,128)}), f32[8,256,1024]{2,1,0:T(8,128)}, u32[]{:S(2)}, u32[]{:S(2)}) %all-to-all-start.1) | async-done | bytes 8388640 | tf_op jit(solution)/shard_map/all_to_all | solution.py:31
  136.6 9.8 %gather_fusion.2 = f32[1024,1024]{1,0:T(8,128)} fusion(f32[2048,1024]{1,0:T(8,128)} %bitcast.8, s32[1024]{0:T(1024)S(1)} %get-tuple-element.6), kind=kCustom, calls=%fused_computation.2 | custom fusion | bytes 8392704 | tf_op jit(solution)/shard_map/gather | solution.py:32
  146.3 2.5 %multiply_reduce_fusion.2 = f32[1024]{0:T(1024)S(1)} fusion(f32[1024,1024]{1,0:T(8,128)} %gather_fusion.2), kind=kLoop, calls=%fused_computation.16 | loop fusion | flops 2096128 | bytes 4198400 | tf_op jit(solution)/shard_map/reduce_sum | solution.py:8
  148.9 26.7 %fusion.21 = (f32[1024]{0:T(1024)S(1)}, f32[1024,8192]{1,0:T(8,128)}) fusion(bf16[8192,1024]{1,0:T(8,128)(2,1)} %param.7, f32[1024,1024]{1,0:T(8,128)} %gather_fusion.2, f32[1024]{0:T(1024)S(1)} %copy-done.2, f32[1024]{0:T(1024)S(1)} %add_rsqrt_fusion.1), kind=kOutput, calls=%fused_computation.64 | convolution fusion | flops 17191403520 | bytes 54538240 | tf_op jit(solution)/shard_map/dot_general | solution.py:42
  175.6 11.9 %pmax.7 = f32[1024]{0:T(1024)S(1)} all-reduce(f32[1024]{0:T(1024)S(1)} %get-tuple-element.17), channel_id=1, replica_groups=mesh['req'=8,'tp'=4] {'tp'}, use_global_device_ids=true, to_apply=%region_8.9 | all-reduce | flops 1024 | bytes 8192 | tf_op jit(solution)/shard_map/pmax | solution.py:46
  187.5 15.2 %fusion = (f32[1024]{0:T(1024)S(1)}, f32[1024]{0:T(1024)S(1)}) fusion(f32[1024,8192]{1,0:T(8,128)} %get-tuple-element.18, f32[1024]{0:T(1024)S(1)} %pmax.7), kind=kLoop, calls=%fused_computation.10 | loop fusion | flops 33552384 | bytes 33566720 | tf_op jit(solution)/shard_map/reduce_sum | solution.py:48
  202.7 15.8 %all-reduce = (f32[2048]{0:T(1024)S(1)}, f32[2,1024]{1,0:T(2,128)S(1)}) all-reduce(f32[2048]{0:T(1024)S(1)} %and_select_fusion, f32[2,1024]{1,0:T(2,128)S(1)} %pad_maximum_fusion), channel_id=1, replica_groups=mesh['req'=8,'tp'=4] {'tp'}, use_global_device_ids=true, to_apply=%region_1.2 | all-reduce | flops 4096 | bytes 32768 | tf_op jit(solution)/shard_map/psum | solution.py:40
  218.6 0.2 copy.15
  218.8 3.3 %scatter_custom_fusion.1 = f32[2,2048]{0,1:T(8,128)S(1)} fusion(s32[1024]{0:T(1024)S(1)} %get-tuple-element.7, f32[1024,2]{1,0:T(8,128)S(1)} %copy.15, f32[]{:T(128)} %constant.27.clone.1), kind=kCustom, calls=%fused_computation.21 | custom fusion | bytes 16388 | tf_op jit(solution)/shard_map/scatter | solution.py:53
  222.2 0.9 copy.16
  223.1 3.3 %all-to-all-start.2 = ((f32[2,8,256]{2,0,1:T(2,128)}), f32[2,8,256]{2,0,1:T(2,128)S(1)}, u32[]{:S(2)}, u32[]{:S(2)}) async-start(f32[2,8,256]{2,0,1:T(2,128)} %copy.16), calls=%async_computation.2 | async-start | bytes 32768 | tf_op jit(solution)/shard_map/all_to_all | solution.py:54
  226.4 8.0 %scatter_custom_fusion.3 = f32[2048]{0:T(1024)S(1)} fusion(s32[2048]{0:T(1024)S(1)} %bitcast.30, f32[2048]{0:T(1024)S(1)} %broadcast.120, f32[]{:T(128)} %constant.27.clone.1), kind=kCustom, calls=%fused_computation.53 | custom fusion | bytes 8196 | tf_op jit(solution)/shard_map/scatter | solution.py:58
  234.5 0.0 all-to-all-done.2
  234.5 8.0 %scatter_custom_fusion.4 = f32[2048]{0:T(1024)S(1)} fusion(s32[2048]{0:T(1024)S(1)} %bitcast.31, f32[2048]{0:T(1024)S(1)} %bitcast.34, f32[]{:T(128)} %constant.27.clone.1), kind=kCustom, calls=%fused_computation.51 | custom fusion | bytes 8196 | tf_op jit(solution)/shard_map/scatter | solution.py:58
  242.6 8.0 %scatter_custom_fusion.2 = f32[2048]{0:T(1024)S(1)} fusion(s32[2048]{0:T(1024)S(1)} %bitcast.32, f32[2048]{0:T(1024)S(1)} %bitcast.33, f32[]{:T(128)} %constant.27.clone.1), kind=kCustom, calls=%fused_computation.55 | custom fusion | bytes 8196 | tf_op jit(solution)/shard_map/scatter | solution.py:58
  250.6 0.6 fusion.20
  (14 shorter events, 0.1 us)
Async XLA Ops:
  37.4 5.3 %copy-start.1 = (s32[2048]{0:T(1024)S(1)}, s32[2048]{0:T(1024)}, u32[]{:S(2)}) copy-start(s32[2048]{0:T(1024)} %param.8) | copy-start | bytes 24580
  37.4 99.2 %all-to-all-start.1 = ((f32[8,256,1024]{2,1,0:T(8,128)}), f32[8,256,1024]{2,1,0:T(8,128)}, u32[]{:S(2)}, u32[]{:S(2)}) async-start(f32[8,256,1024]{2,1,0:T(8,128)} %broadcast_select_fusion), calls=%async_computation.1 | async-start | bytes 16777216 | tf_op jit(solution)/shard_map/all_to_all | solution.py:31
  61.7 4.6 %copy-start = (bf16[2048,1024]{1,0:T(8,128)(2,1)S(1)}, bf16[2048,1024]{1,0:T(8,128)(2,1)}, u32[]{:S(2)}) copy-start(bf16[2048,1024]{1,0:T(8,128)(2,1)} %gather_fusion) | copy-start | bytes 12582916
  61.7 4.6 %copy-start.2 = (f32[1024]{0:T(1024)S(1)}, f32[1024]{0:T(1024)}, u32[]{:S(2)}) copy-start(f32[1024]{0:T(1024)} %param.6) | copy-start | bytes 12292
  223.1 11.4 %all-to-all-start.2 = ((f32[2,8,256]{2,0,1:T(2,128)}), f32[2,8,256]{2,0,1:T(2,128)S(1)}, u32[]{:S(2)}, u32[]{:S(2)}) async-start(f32[2,8,256]{2,0,1:T(2,128)} %copy.16), calls=%async_computation.2 | async-start | bytes 32768 | tf_op jit(solution)/shard_map/all_to_all | solution.py:54
where the time goes:
time: 252 us; the launch traced here: 251 us
  local copies, waits for them, and re-layouts  77.2 us (31%)
  waiting for transfers between devices  66 us (26%)
  blocking collectives  37.4 us (15%)
  other arithmetic  34.6 us (14%)
  matrix products  26.7 us (11%)
  starting transfers between devices  8.61 us (3%)
    all_to_all x1, waiting for transfers between devices, body(): lax.all_to_all(outgoing_rows, 'req', split_axis=0, concat_axis=0, tiled=T...  66 us
    dot_general x1, matrix products, body(): lax.dot_general(normed, embedding, (((1,), (1,)), ((), ())), preferred_el...  26.7 us
    scatter x3, local copies, waits for them, and re-layouts, to_owner(): jnp.zeros((own_rows,), jnp.float32).at[home_row].set(values, mode='drop')  24.1 us
    gather x1, local copies, waits for them, and re-layouts, body(): target_rows = embedding[jnp.clip(in_shard_id, 0, shard_cols - 1)]  18.9 us
    psum x1, blocking collectives, body(): owner_chosen = lax.psum(jnp.where(inside, target_term, 0.0), 'tp')  15.8 us
    reduce_sum x1, other arithmetic, body(): jnp.sum(weights, axis=1)  15.2 us
    gather x1, local copies, waits for them, and re-layouts, body(): outgoing_rows = jnp.where(is_live[:, None], final_states[picked], 0.0)  15.1 us
    pmax x1, blocking collectives, body(): row_peak = lax.pmax(local_peak, 'tp')  11.9 us
  transfers between devices with their start and end apart: 2, of which 1 were waited for; matrix products, arithmetic and copies ran while one was open for 14% of the time, Pallas kernels for 0%

commit v1 on v0

--- a/solution.py
+++ b/solution.py
@@ -24,7 +24,19 @@
     offset = jnp.arange(positions, dtype=jnp.int32) - jnp.sum(member * starts[None, :], axis=1)
     slot_index = source * capacity + offset
     asked_rows = jnp.full((owners * capacity,), -1, jnp.int32).at[slot_index].set(local_row)
-    wanted = lax.all_to_all(asked_rows, "req", split_axis=0, concat_axis=0, tiled=True)
+    ways, here = (lax.axis_size("req"), lax.axis_index("req"))
+    width = asked_rows.shape[0] // ways
+    dims = list(asked_rows.shape)
+    dims[0] = width
+    height = dims[0]
+    dims[0] = height * ways
+    full = jnp.zeros(dims, asked_rows.dtype)
+    for mask in range(ways):
+        part = lax.dynamic_slice_in_dim(asked_rows, (here ^ mask) * width, width, axis=0)
+        if mask:
+            part = lax.ppermute(part, "req", [(d, d ^ mask) for d in range(ways)])
+        full = lax.dynamic_update_slice_in_dim(full, part, (here ^ mask) * height, axis=0)
+    wanted = full
     is_live = wanted >= 0
     picked = jnp.where(is_live, wanted, 0)
     outgoing_rows = jnp.where(is_live[:, None], final_states[picked], 0.0)

time: 252 us -> 254 us (level)
  blocking collectives: 37.4 us -> 27.7 us
  starting transfers between devices: 8.61 us -> 16.2 us
    all_to_all x1 -> x0, blocking collectives: 9.67 us -> none  [body(): lax.all_to_all(asked_rows, 'req', split_axis=0, concat_axis=0, tiled=True)]
    ppermute x0 -> x7, starting transfers between devices: none -> 7.61 us  [body(): part = lax.ppermute(part, 'req', [(d, d ^ mask) for d in range(ways)])]
    select_n x2 -> x1, other arithmetic: 5.82 us -> 5.78 us  [body(): outgoing_rows = jnp.where(is_live[:, None], final_states[picked], 0.0)]
  transfers between devices with their start and end apart: 2 -> 9, of which waited for: 1 -> 3; matrix products, arithmetic and copies ran while one was open for 14% -> 15% of each run, Pallas kernels for 0% -> 0%
where the time goes in v1:
time: 254 us; the launch traced here: 253 us
  local copies, waits for them, and re-layouts  78.9 us (31%)
  waiting for transfers between devices  68.4 us (27%)
  other arithmetic  34.5 us (14%)
  blocking collectives  27.7 us (11%)
  matrix products  26.7 us (11%)
  starting transfers between devices  16.2 us (6%)
    all_to_all x1, waiting for transfers between devices, body(): lax.all_to_all(outgoing_rows, 'req', split_axis=0, concat_axis=0, tiled=T...  66 us
    dot_general x1, matrix products, body(): lax.dot_general(normed, embedding, (((1,), (1,)), ((), ())), preferred_el...  26.7 us
    scatter x3, local copies, waits for them, and re-layouts, to_owner(): jnp.zeros((own_rows,), jnp.float32).at[home_row].set(values, mode='drop')  24.1 us
    gather x1, local copies, waits for them, and re-layouts, body(): target_rows = embedding[jnp.clip(in_shard_id, 0, shard_cols - 1)]  18.9 us
    psum x1, blocking collectives, body(): owner_chosen = lax.psum(jnp.where(inside, target_term, 0.0), 'tp')  15.8 us
    reduce_sum x1, other arithmetic, body(): jnp.sum(weights, axis=1)  15.2 us
    gather x1, local copies, waits for them, and re-layouts, body(): outgoing_rows = jnp.where(is_live[:, None], final_states[picked], 0.0)  15.1 us
    pmax x1, blocking collectives, body(): row_peak = lax.pmax(local_peak, 'tp')  11.9 us
  transfers between devices with their start and end apart: 9, of which 3 were waited for; matrix products, arithmetic and copies ran while one was open for 15% of the time, Pallas kernels for 0%

profile of v1, /device:TPU:0, one launch (start us, length us, event | category | flops | bytes accessed | tf_op | source)
XLA Modules:
  0.0 253.4 jit_solution(16585578204541953268)
XLA Ops:
  0.7 0.7 add_select_fusion.1
  1.4 0.1 convert_reduce_fusion
  1.5 0.2 reduce-window.8
  1.7 0.1 select_reduce_fusion
  1.8 0.7 broadcast_clamp_fusion
  2.5 4.3 %scatter_custom_fusion = s32[2048]{0:T(1024)S(1)} fusion(s32[1024]{0:T(1024)S(1)} %get-tuple-element.7, s32[1024]{0:T(1024)S(1)} %get-tuple-element.24, s32[]{:T(128)} %constant.31.clone.1), kind=kCustom, calls=%fused_computation.45 | custom fusion | bytes 8196 | tf_op jit(solution)/shard_map/scatter | solution.py:26
  6.8 0.2 fusion.21
  7.1 0.5 collective-permute-start
  7.5 2.6 %collective-permute-start.1 = (s32[256]{0:T(256)S(1)}, s32[256]{0:T(256)S(1)}, u32[]{:S(2)}, u32[]{:S(2)}) collective-permute-start(s32[256]{0:T(256)S(1)} %get-tuple-element.21), channel_id=1, source_target_pairs={{0,8},{4,12},{8,0},{12,4},{16,24},{20,28},{24,16},{28,20},{1,9},{5... | collective-permute-start | bytes 3080 | tf_op jit(solution)/shard_map/ppermute | solution.py:37
  10.1 0.1 collective-permute-start.2
  10.2 1.8 collective-permute-start.3
  11.9 0.0 collective-permute-start.4
  11.9 0.0 collective-permute-done
  11.9 2.6 %collective-permute-start.5 = (s32[256]{0:T(256)S(1)}, s32[256]{0:T(256)S(1)}, u32[]{:S(2)}, u32[]{:S(2)}) collective-permute-start(s32[256]{0:T(256)S(1)} %get-tuple-element.17), channel_id=1, source_target_pairs={{0,24},{4,28},{8,16},{12,20},{16,8},{20,12},{24,0},{28,4},{1,25},{... | collective-permute-start | bytes 3080 | tf_op jit(solution)/shard_map/ppermute | solution.py:37
  14.6 0.0 collective-permute-done.1
  14.6 0.1 collective-permute-start.6
  14.7 0.2 dynamic_update_slice.25
  14.9 0.3 dynamic_update_slice.26
  15.1 0.0 collective-permute-done.2
  15.1 0.3 dynamic_update_slice.27
  15.4 0.0 collective-permute-done.3
  15.4 0.2 dynamic_update_slice.28
  15.6 0.0 collective-permute-done.4
  15.6 0.2 dynamic_update_slice.29
  15.8 0.6 collective-permute-done.5
  16.4 0.2 dynamic_update_slice.30
  16.6 1.8 collective-permute-done.6
  18.5 0.2 dynamic_update_slice.31
  18.7 15.1 %gather_fusion.1 = f32[2048,1024]{1,0:T(8,128)} fusion(f32[2048,1024]{1,0:T(8,128)} %param.5, s32[2048]{0:T(1024)S(1)} %get-tuple-element.14), kind=kCustom, calls=%fused_computation.1 | custom fusion | bytes 16785408 | tf_op jit(solution)/shard_map/gather | solution.py:42
  33.8 5.8 %broadcast_select_fusion = f32[8,256,1024]{2,1,0:T(8,128)} fusion(f32[8,256,1024]{2,1,0:T(8,128)} %bitcast.15, pred[8,256]{1,0:T(8,128)(4,1)S(1)} %broadcast_in_dim.64), kind=kLoop, calls=%fused_computation.17 | loop fusion | flops 2097152 | bytes 16779264 | tf_op jit(solution)/shard_map/jit(_where)/select_n | solution.py:42
  39.6 0.0 copy-start.1
  39.6 5.3 %all-to-all-start = ((f32[8,256,1024]{2,1,0:T(8,128)}), f32[8,256,1024]{2,1,0:T(8,128)}, u32[]{:S(2)}, u32[]{:S(2)}) async-start(f32[8,256,1024]{2,1,0:T(8,128)} %broadcast_select_fusion), calls=%async_computation | async-start | bytes 16777216 | tf_op jit(solution)/shard_map/all_to_all | solution.py:43
  44.9 0.0 copy-done.1
  44.9 18.9 %gather_fusion = bf16[2048,1024]{1,0:T(8,128)(2,1)} fusion(bf16[8192,1024]{1,0:T(8,128)(2,1)} %param.7, s32[2048]{0:T(1024)S(1)} %fusion.7), kind=kCustom, calls=%fused_computation | custom fusion | bytes 8396800 | tf_op jit(solution)/shard_map/gather | solution.py:48
  63.8 0.0 copy-start
  63.8 0.0 copy-start.2
  63.8 4.1 %multiply_reduce_fusion.1 = f32[2048]{0:T(1024)S(1)} fusion(f32[2048,1024]{1,0:T(8,128)} %param.5), kind=kLoop, calls=%fused_computation.14 | loop fusion | flops 4192256 | bytes 8396800 | tf_op jit(solution)/shard_map/reduce_sum | solution.py:8
  68.0 0.4 copy-done
  68.4 0.0 copy-done.2
  68.4 4.4 %fusion.1 = f32[2048]{0:T(1024)S(1)} fusion(bf16[2048,1024]{1,0:T(8,128)(2,1)S(1)} %copy-done, f32[2048,1024]{1,0:T(8,128)} %param.5, f32[1024]{0:T(1024)S(1)} %copy-done.2, f32[2048]{0:T(1024)S(1)} %add_rsqrt_fusion), kind=kLoop, calls=%fused_computation.12 | loop fusion | flops 14678016 | bytes 12603392 | tf_op jit(solution)/shard_map/rd,rd->r/dot_general | solution.py:49
  72.8 66.0 %all-to-all-done = f32[8,256,1024]{2,1,0:T(8,128)} async-done(((f32[8,256,1024]{2,1,0:T(8,128)}), f32[8,256,1024]{2,1,0:T(8,128)}, u32[]{:S(2)}, u32[]{:S(2)}) %all-to-all-start) | async-done | bytes 8388640 | tf_op jit(solution)/shard_map/all_to_all | solution.py:43
  138.8 9.8 %gather_fusion.2 = f32[1024,1024]{1,0:T(8,128)} fusion(f32[2048,1024]{1,0:T(8,128)} %bitcast.3, s32[1024]{0:T(1024)S(1)} %get-tuple-element.6), kind=kCustom, calls=%fused_computation.2 | custom fusion | bytes 8392704 | tf_op jit(solution)/shard_map/gather | solution.py:44
  148.5 2.5 multiply_reduce_fusion.2
  151.1 26.7 %fusion.22 = (f32[1024]{0:T(1024)S(1)}, f32[1024,8192]{1,0:T(8,128)}) fusion(bf16[8192,1024]{1,0:T(8,128)(2,1)} %param.7, f32[1024,1024]{1,0:T(8,128)} %gather_fusion.2, f32[1024]{0:T(1024)S(1)} %copy-done.2, f32[1024]{0:T(1024)S(1)} %add_rsqrt_fusion.1), kind=kOutput, calls=%fused_computation.63 | convolution fusion | flops 17191403520 | bytes 54538240 | tf_op jit(solution)/shard_map/dot_general | solution.py:54
  177.7 11.9 %pmax.7 = f32[1024]{0:T(1024)S(1)} all-reduce(f32[1024]{0:T(1024)S(1)} %get-tuple-element.25), channel_id=1, replica_groups=mesh['req'=8,'tp'=4] {'tp'}, use_global_device_ids=true, to_apply=%region_8.9 | all-reduce | flops 1024 | bytes 8192 | tf_op jit(solution)/shard_map/pmax | solution.py:58
  189.7 15.2 %fusion = (f32[1024]{0:T(1024)S(1)}, f32[1024]{0:T(1024)S(1)}) fusion(f32[1024,8192]{1,0:T(8,128)} %get-tuple-element.26, f32[1024]{0:T(1024)S(1)} %pmax.7), kind=kLoop, calls=%fused_computation.10 | loop fusion | flops 33552384 | bytes 33566720 | tf_op jit(solution)/shard_map/reduce_sum | solution.py:60
  204.9 15.8 %all-reduce = (f32[2048]{0:T(1024)S(1)}, f32[2,1024]{1,0:T(2,128)S(1)}) all-reduce(f32[2048]{0:T(1024)S(1)} %and_select_fusion, f32[2,1024]{1,0:T(2,128)S(1)} %pad_maximum_fusion), channel_id=1, replica_groups=mesh['req'=8,'tp'=4] {'tp'}, use_global_device_ids=true, to_apply=%region_1.2 | all-reduce | flops 4096 | bytes 32768 | tf_op jit(solution)/shard_map/psum | solution.py:52
  220.7 0.2 copy.11
  221.0 3.3 %scatter_custom_fusion.1 = f32[2,2048]{0,1:T(8,128)S(1)} fusion(s32[1024]{0:T(1024)S(1)} %get-tuple-element.7, f32[1024,2]{1,0:T(8,128)S(1)} %copy.11, f32[]{:T(128)} %constant.27.clone.1), kind=kCustom, calls=%fused_computation.21 | custom fusion | bytes 16388 | tf_op jit(solution)/shard_map/scatter | solution.py:65
  224.3 0.9 copy.12
  225.2 3.3 %all-to-all-start.1 = ((f32[2,8,256]{2,0,1:T(2,128)}), f32[2,8,256]{2,0,1:T(2,128)S(1)}, u32[]{:S(2)}, u32[]{:S(2)}) async-start(f32[2,8,256]{2,0,1:T(2,128)} %copy.12), calls=%async_computation.1 | async-start | bytes 32768 | tf_op jit(solution)/shard_map/all_to_all | solution.py:66
  228.6 8.0 %scatter_custom_fusion.3 = f32[2048]{0:T(1024)S(1)} fusion(s32[2048]{0:T(1024)S(1)} %get-tuple-element.15, f32[2048]{0:T(1024)S(1)} %broadcast.59, f32[]{:T(128)} %constant.27.clone.1), kind=kCustom, calls=%fused_computation.49 | custom fusion | bytes 8196 | tf_op jit(solution)/shard_map/scatter | solution.py:70
  236.7 0.0 all-to-all-done.1
  236.7 8.0 %scatter_custom_fusion.4 = f32[2048]{0:T(1024)S(1)} fusion(s32[2048]{0:T(1024)S(1)} %get-tuple-element.15, f32[2048]{0:T(1024)S(1)} %bitcast.22, f32[]{:T(128)} %constant.27.clone.1), kind=kCustom, calls=%fused_computation.47 | custom fusion | bytes 8196 | tf_op jit(solution)/shard_map/scatter | solution.py:70
  244.7 8.0 %scatter_custom_fusion.2 = f32[2048]{0:T(1024)S(1)} fusion(s32[2048]{0:T(1024)S(1)} %get-tuple-element.15, f32[2048]{0:T(1024)S(1)} %bitcast.21, f32[]{:T(128)} %constant.27.clone.1), kind=kCustom, calls=%fused_computation.51 | custom fusion | bytes 8196 | tf_op jit(solution)/shard_map/scatter | solution.py:70
  252.8 0.6 fusion.20
  (15 shorter events, 0.1 us)
Async XLA Ops:
  7.1 4.9 %collective-permute-start = (s32[256]{0:T(256)S(1)}, s32[256]{0:T(256)S(1)}, u32[]{:S(2)}, u32[]{:S(2)}) collective-permute-start(s32[256]{0:T(256)S(1)} %get-tuple-element.22), channel_id=1, source_target_pairs={{0,4},{4,0},{8,12},{12,8},{16,20},{20,16},{24,28},{28,24},{1,5},{5... | collective-permute-start | bytes 3080 | tf_op jit(solution)/shard_map/ppermute | solution.py:37
  7.5 7.0 %collective-permute-start.1 = (s32[256]{0:T(256)S(1)}, s32[256]{0:T(256)S(1)}, u32[]{:S(2)}, u32[]{:S(2)}) collective-permute-start(s32[256]{0:T(256)S(1)} %get-tuple-element.21), channel_id=1, source_target_pairs={{0,8},{4,12},{8,0},{12,4},{16,24},{20,28},{24,16},{28,20},{1,9},{5... | collective-permute-start | bytes 3080 | tf_op jit(solution)/shard_map/ppermute | solution.py:37
  10.1 5.0 %collective-permute-start.2 = (s32[256]{0:T(256)S(1)}, s32[256]{0:T(256)S(1)}, u32[]{:S(2)}, u32[]{:S(2)}) collective-permute-start(s32[256]{0:T(256)S(1)} %get-tuple-element.20), channel_id=1, source_target_pairs={{0,12},{4,8},{8,4},{12,0},{16,28},{20,24},{24,20},{28,16},{1,13},{... | collective-permute-start | bytes 3080 | tf_op jit(solution)/shard_map/ppermute | solution.py:37
  10.2 5.2 %collective-permute-start.3 = (s32[256]{0:T(256)S(1)}, s32[256]{0:T(256)S(1)}, u32[]{:S(2)}, u32[]{:S(2)}) collective-permute-start(s32[256]{0:T(256)S(1)} %get-tuple-element.19), channel_id=1, source_target_pairs={{0,16},{4,20},{8,24},{12,28},{16,0},{20,4},{24,8},{28,12},{1,17},{... | collective-permute-start | bytes 3080 | tf_op jit(solution)/shard_map/ppermute | solution.py:37
  11.9 3.7 %collective-permute-start.4 = (s32[256]{0:T(256)S(1)}, s32[256]{0:T(256)S(1)}, u32[]{:S(2)}, u32[]{:S(2)}) collective-permute-start(s32[256]{0:T(256)S(1)} %get-tuple-element.18), channel_id=1, source_target_pairs={{0,20},{4,16},{8,28},{12,24},{16,4},{20,0},{24,12},{28,8},{1,21},{... | collective-permute-start | bytes 3080 | tf_op jit(solution)/shard_map/ppermute | solution.py:37
  11.9 4.5 %collective-permute-start.5 = (s32[256]{0:T(256)S(1)}, s32[256]{0:T(256)S(1)}, u32[]{:S(2)}, u32[]{:S(2)}) collective-permute-start(s32[256]{0:T(256)S(1)} %get-tuple-element.17), channel_id=1, source_target_pairs={{0,24},{4,28},{8,16},{12,20},{16,8},{20,12},{24,0},{28,4},{1,25},{... | collective-permute-start | bytes 3080 | tf_op jit(solution)/shard_map/ppermute | solution.py:37
  14.6 3.9 %collective-permute-start.6 = (s32[256]{0:T(256)S(1)}, s32[256]{0:T(256)S(1)}, u32[]{:S(2)}, u32[]{:S(2)}) collective-permute-start(s32[256]{0:T(256)S(1)} %get-tuple-element.16), channel_id=1, source_target_pairs={{0,28},{4,24},{8,20},{12,16},{16,12},{20,8},{24,4},{28,0},{1,29},{... | collective-permute-start | bytes 3080 | tf_op jit(solution)/shard_map/ppermute | solution.py:37
  39.6 5.3 %copy-start.1 = (s32[2048]{0:T(1024)S(1)}, s32[2048]{0:T(1024)}, u32[]{:S(2)}) copy-start(s32[2048]{0:T(1024)} %param.8) | copy-start | bytes 24580
  39.6 99.2 %all-to-all-start = ((f32[8,256,1024]{2,1,0:T(8,128)}), f32[8,256,1024]{2,1,0:T(8,128)}, u32[]{:S(2)}, u32[]{:S(2)}) async-start(f32[8,256,1024]{2,1,0:T(8,128)} %broadcast_select_fusion), calls=%async_computation | async-start | bytes 16777216 | tf_op jit(solution)/shard_map/all_to_all | solution.py:43
  63.8 4.6 %copy-start = (bf16[2048,1024]{1,0:T(8,128)(2,1)S(1)}, bf16[2048,1024]{1,0:T(8,128)(2,1)}, u32[]{:S(2)}) copy-start(bf16[2048,1024]{1,0:T(8,128)(2,1)} %gather_fusion) | copy-start | bytes 12582916
  63.8 4.6 %copy-start.2 = (f32[1024]{0:T(1024)S(1)}, f32[1024]{0:T(1024)}, u32[]{:S(2)}) copy-start(f32[1024]{0:T(1024)} %param.6) | copy-start | bytes 12292
  225.2 11.4 %all-to-all-start.1 = ((f32[2,8,256]{2,0,1:T(2,128)}), f32[2,8,256]{2,0,1:T(2,128)S(1)}, u32[]{:S(2)}, u32[]{:S(2)}) async-start(f32[2,8,256]{2,0,1:T(2,128)} %copy.12), calls=%async_computation.1 | async-start | bytes 32768 | tf_op jit(solution)/shard_map/all_to_all | solution.py:66
